TPU v7x, 512 devices: a whole 4x4x16 slice. The times are simulated.
512 devices in a mesh: ctx: 32 (over z_hi, y, x), exp: 16 (over z_lo, core).
Axes of the slice: x: 4, y: 4, z: 16 (z_hi: 2, z_lo: 8; z = z_hi * 8 + z_lo), core: 2. Of those that a mesh axis runs over, the one named last changes fastest.
Arguments:
- hidden_in: bfloat16 [4096, 2880], P('ctx'), may hold values from -6 to 6
- query_input: bfloat16 [4096, 2048], P('ctx', 'exp'), may hold values from -16 to 16
- key_heads_input: bfloat16 [4096, 256], P('ctx'), may hold values from -16 to 16
- value_heads_input: bfloat16 [4096, 256], P('ctx'), may hold values from -6 to 6
- sink_logits: float32 [32], P('exp'), may hold values from 0 to 4
- out_proj: bfloat16 [2048, 2880], P('exp'), may hold values from -0.125 to 0.125
- norm_gain: float32 [2880], replicated, may hold values from 0.5 to 1.5
- expert_ids: int32 [4096, 4], P('ctx'), may hold values from 0 to 31, all different within a row; in each aligned block of 128 rows (0 to 127, 128 to 255, ...) at most 20 rows name the same one
- expert_gates: float32 [4096, 4], P('ctx'), may hold values from 0.1 to 1
- gate_up: bfloat16 [32, 2880, 2, 2880], P('ctx', None, None, 'exp'), may hold values from -0.109375 to 0.109375
- down_proj: bfloat16 [32, 2880, 2880], P('ctx', 'exp'), may hold values from -0.109375 to 0.109375
Outputs:
- layer_out: bfloat16 [4096, 2880], P('ctx', 'exp')
Inputs may be any that keep to these rules, and one draw needn't show every extreme that they name: `expert_ids`: each token names 4 different experts; within the 128 tokens of one device no expert is named by more than 20 tokens.
All inputs are finite; a program needn't handle non-finite values.
Results may differ from a plain program's by a relative error of at most 0.02.
Values may be sent and summed in bfloat16 or wider, within the bound.
No kernel may reach another device: no remote copies, remote signals or barrier semaphores. Data moves between devices by JAX's collectives and lax.ppermute only.
A program may use at most 64 MiB of HBM per device.

v0:
```python
import functools
import math
import jax
import jax.numpy as jnp
import numpy as np
from jax import lax
from jax.sharding import Mesh, PartitionSpec as P

D = 2880
QUERY_HEADS = 32
KEY_VALUE_HEADS = 4
HEAD_SIZE = 64
yarn_base = 150000.0
yarn_factor = 32.0
yarn_initial = 4096.0
beta_fast = 32.0
beta_slow = 1.0
neg_large = -1e30


def yarn_frequencies(head_dim):
    half_dim = head_dim // 2

    def correction(rotations):
        return (
            head_dim
            * math.log(yarn_initial / (rotations * 2.0 * math.pi))
            / (2.0 * math.log(yarn_base))
        )

    lower_dim = max(math.floor(correction(beta_fast)), 0)
    upper_dim = min(math.ceil(correction(beta_slow)), head_dim - 1)
    extrap_freq = 1.0 / yarn_base ** (np.arange(0, head_dim, 2) / head_dim)
    interp_freq = extrap_freq / yarn_factor
    ramp_part = np.clip((np.arange(half_dim) - lower_dim) / (upper_dim - lower_dim), 0.0, 1.0)
    extrap_share = 1.0 - ramp_part
    return (interp_freq * (1.0 - extrap_share) + extrap_freq * extrap_share).astype(np.float32)


def rotate_with_yarn(heads_in, token_positions):
    head_dim = heads_in.shape[-1]
    freqs = jnp.asarray(yarn_frequencies(head_dim))
    angles = token_positions.astype(jnp.float32)[:, None] * freqs[None, :]
    factor = 0.1 * math.log(yarn_factor) + 1.0
    cosine = (jnp.cos(angles) * factor)[:, None, :]
    sine = (jnp.sin(angles) * factor)[:, None, :]
    first_half = heads_in[..., : head_dim // 2]
    second_half = heads_in[..., head_dim // 2 :]
    return jnp.concatenate(
        [first_half * cosine - second_half * sine, second_half * cosine + first_half * sine],
        axis=-1,
    )


def route_slots(ids_block, n_experts):
    flat_ids = ids_block.reshape(-1)
    onehot = (flat_ids[:, None] == jnp.arange(n_experts, dtype=jnp.int32)[None, :]).astype(
        jnp.int32
    )
    ranks = jnp.cumsum(onehot, axis=0) - onehot
    return jnp.sum(ranks * onehot, axis=1).reshape(ids_block.shape)


CTX = ("zh", "y", "x")
EXP = ("zl", "c")


def per_device(
    hidden_in,
    query_input,
    key_heads_input,
    value_heads_input,
    sink_logits,
    out_proj,
    norm_gain,
    expert_ids,
    expert_gates,
    gate_up,
    down_proj,
    *,
    ctx_count,
    zl_count,
    c_count
):
    tok_rows = hidden_in.shape[0]
    exp_count = zl_count * c_count
    local_heads = query_input.shape[1] // HEAD_SIZE
    ctx_index = lax.axis_index(CTX)
    exp_index = lax.axis_index(EXP)
    token_positions = ctx_index * tok_rows + jnp.arange(tok_rows, dtype=jnp.int32)
    q_rot = rotate_with_yarn(
        query_input.astype(jnp.float32).reshape(tok_rows, local_heads, HEAD_SIZE), token_positions
    ).astype(jnp.bfloat16)
    shared_key_head = exp_index * local_heads // (QUERY_HEADS // KEY_VALUE_HEADS)
    key_block = lax.dynamic_slice_in_dim(key_heads_input, shared_key_head * HEAD_SIZE, HEAD_SIZE, 1)
    value_block = lax.dynamic_slice_in_dim(
        value_heads_input, shared_key_head * HEAD_SIZE, HEAD_SIZE, 1
    )
    key_rot = (
        rotate_with_yarn(
            key_block.astype(jnp.float32).reshape(tok_rows, 1, HEAD_SIZE), token_positions
        )
        .reshape(tok_rows, HEAD_SIZE)
        .astype(jnp.bfloat16)
    )
    key_value = jnp.concatenate([key_rot, value_block], axis=1)
    score_scale = 1.0 / math.sqrt(HEAD_SIZE)
    block_part = lax.all_gather(key_value, CTX, axis=0, tiled=True)
    run_max = jnp.broadcast_to(sink_logits[:, None], (local_heads, tok_rows))
    run_total = jnp.ones((local_heads, tok_rows), jnp.float32)
    key_count = block_part.shape[0]
    key_part = block_part[:, :HEAD_SIZE]
    value_part = block_part[:, HEAD_SIZE:].astype(jnp.float32)
    scores = (
        jnp.einsum("rhd,kd->hrk", q_rot, key_part, preferred_element_type=jnp.float32) * score_scale
    )
    key_pos = jnp.arange(key_count, dtype=jnp.int32)
    visible = token_positions[:, None] >= key_pos[None, :]
    scores = jnp.where(visible[None, :, :], scores, neg_large)
    new_max = jnp.maximum(run_max, jnp.max(scores, axis=2))
    weights = jnp.exp(scores - new_max[:, :, None])
    factor = jnp.exp(run_max - new_max)
    run_total = run_total * factor + jnp.sum(weights, axis=2)
    run_sum = jnp.einsum("hrk,kd->hrd", weights, value_part, precision=lax.Precision.HIGHEST)
    attended = (
        (run_sum / run_total[:, :, None])
        .transpose(1, 0, 2)
        .reshape(tok_rows, local_heads * HEAD_SIZE)
        .astype(jnp.bfloat16)
    )
    col_width = D // exp_count
    head_part = jnp.dot(attended, out_proj, preferred_element_type=jnp.float32).astype(jnp.bfloat16)
    head_part = head_part.reshape(tok_rows, zl_count, c_count, col_width).transpose(2, 1, 0, 3)
    head_part = lax.psum_scatter(head_part, "c", scatter_dimension=0, tiled=True)[0]
    head_cols = lax.psum_scatter(head_part, "zl", scatter_dimension=0, tiled=True)[0]
    residual_cols = lax.dynamic_slice_in_dim(hidden_in, exp_index * col_width, col_width, 1).astype(
        jnp.float32
    ) + head_cols.astype(jnp.float32)
    square_sum = lax.psum(jnp.sum(residual_cols * residual_cols, axis=1), EXP)
    gain_cols = lax.dynamic_slice_in_dim(norm_gain, exp_index * col_width, col_width, 0)
    normed_cols = (
        residual_cols * lax.rsqrt(square_sum / D + 1e-05)[:, None] * gain_cols[None, :]
    ).astype(jnp.bfloat16)
    exp_local = gate_up.shape[0]
    n_experts = exp_local * ctx_count
    top_count = expert_ids.shape[1]
    capacity = max(2, tok_rows * top_count * 5 // (4 * n_experts))
    slot_index = route_slots(expert_ids, n_experts)
    dest_row = expert_ids * capacity + slot_index
    spread_rows = jnp.broadcast_to(
        normed_cols[:, None, :], (tok_rows, top_count, col_width)
    ).reshape(tok_rows * top_count, col_width)
    send_rows = (
        jnp.zeros((n_experts * capacity, col_width), jnp.bfloat16)
        .at[dest_row.reshape(-1)]
        .set(spread_rows)
    )
    bucket_rows = ctx_count * capacity
    unit_count = gate_up.shape[-1]
    received = lax.all_to_all(
        send_rows.reshape(ctx_count, exp_local * capacity, col_width),
        CTX,
        split_axis=0,
        concat_axis=0,
        tiled=True,
    ).reshape(bucket_rows, col_width)
    gathered = lax.all_gather(received, "zl", axis=0, tiled=False)
    gathered = lax.all_gather(gathered, "c", axis=0, tiled=False)
    weights_flat = gate_up.reshape(zl_count, c_count, col_width, 2 * unit_count)
    gate_up_out = jnp.einsum(
        "czrk,zckf->rf", gathered, weights_flat, preferred_element_type=jnp.float32
    )
    gate_up_out = gate_up_out.reshape(bucket_rows, 2, unit_count)
    gate_value = gate_up_out[:, 0]
    up_value = gate_up_out[:, 1]
    activated = ((up_value + 1.0) * gate_value * jax.nn.sigmoid(1.702 * gate_value)).astype(
        jnp.bfloat16
    )
    down_local = down_proj.reshape(unit_count, zl_count, c_count, col_width)
    partial_value = jnp.einsum(
        "rf,fzcd->czrd", activated, down_local, preferred_element_type=jnp.float32
    ).astype(jnp.bfloat16)
    partial_value = lax.psum_scatter(partial_value, "c", scatter_dimension=0, tiled=True)[0]
    expert_cols = lax.psum_scatter(partial_value, "zl", scatter_dimension=0, tiled=True)[0]
    returned = lax.all_to_all(
        expert_cols.reshape(ctx_count, capacity, col_width),
        CTX,
        split_axis=0,
        concat_axis=0,
        tiled=True,
    )
    picked_rows = returned.reshape(n_experts * capacity, col_width)[dest_row]
    moe_cols = jnp.sum(expert_gates[:, :, None] * picked_rows.astype(jnp.float32), axis=1)
    return (residual_cols + moe_cols).astype(jnp.bfloat16)


def solution(mesh):
    ctx_count, exp_count = mesh.devices.shape
    zh, y, x = (mesh.devices.shape[0] // 16, 4, 4)
    c_count = 2
    zl_count = exp_count // c_count
    fine = Mesh(mesh.devices.reshape(zh, y, x, zl_count, c_count), ("zh", "y", "x", "zl", "c"))
    placed = (
        P(CTX, None),
        P(CTX, EXP),
        P(CTX, None),
        P(CTX, None),
        P(EXP),
        P(EXP, None),
        P(),
        P(CTX, None),
        P(CTX, None),
        P(CTX, None, None, EXP),
        P(CTX, EXP, None),
    )
    return jax.shard_map(
        functools.partial(per_device, ctx_count=ctx_count, zl_count=zl_count, c_count=c_count),
        mesh=fine,
        in_specs=placed,
        out_specs=P(CTX, EXP),
        check_vma=False,
    )
```

profile of v0, /device:TPU:32, one launch (start us, length us, event | category | flops | bytes accessed | tf_op | source)
XLA Modules:
  0.0 534.8 jit_solution(13582523231836904942)
XLA Ops:
  6.5 0.9 constant_dynamic-slice_fusion
  7.7 0.8 fusion.33
  8.5 0.6 pad_maximum_fusion
  9.2 0.8 copy.67
  10.1 0.8 fusion.39
  10.9 0.3 iota_compare_fusion
  11.3 113.0 %all-gather.5.cloned.1.call-done = bf16[4096,128]{0,1:T(8,128)(2,1)} async-done(((bf16[128,128]{0,1:T(8,128)(2,1)}), bf16[4096,128]{0,1:T(8,128)(2,1)}) %all-gather.5.cloned.1.call-update) | async-done | bytes 1048592 | tf_op jit(solution)/shard_map/all_gather | solution.py:108
  124.3 2.0 fusion.45
  126.4 0.6 fusion.2
  127.0 2.1 fusion.13
  129.1 0.3 convolution_convert_fusion
  129.4 0.1 reshape.307
  129.6 1.1 copy.69
  130.7 0.1 copy.73
  130.8 0.1 eq.29
  130.9 0.1 eq.25
  131.1 16.4 %reduce-scatter.11.cloned.1.call-done = bf16[1,8,128,180]{2,1,3,0:T(8,128)(2,1)} async-done(((bf16[2,8,128,180]{2,1,3,0:T(8,128)(2,1)}), bf16[1,8,128,180]{2,1,3,0:T(8,128)(2,1)}) %reduce-scatter.11.cloned.1.call-update) | async-done | bytes 368656 | tf_op jit(solution)/shard_map/reduce_scatter | solution.py:134
  147.5 1.8 copy.70
  149.3 0.8 constant_dynamic-slice_fusion.2
  150.1 0.1 copy.96
  150.2 0.8 dynamic_slice.15
  151.0 1.1 reduce-window.6
  152.2 0.2 slice_reduce_fusion
  152.4 0.1 fusion.24
  152.5 0.1 reshape.309
  152.7 0.1 copy.77
  152.9 0.1 reshape.310
  153.0 55.7 %reduce-scatter.15.cloned.1.call-done = bf16[1,128,180]{1,2,0:T(8,128)(2,1)} async-done(((bf16[8,128,180]{1,2,0:T(8,128)(2,1)}), bf16[1,128,180]{1,2,0:T(8,128)(2,1)}) %reduce-scatter.15.cloned.1.call-update) | async-done | bytes 46096
  208.7 0.9 copy.71
  209.6 0.1 multiply_reduce_fusion.1
  209.7 44.4 %psum.7 = f32[128]{0:T(128)S(1)} all-reduce(f32[128]{0:T(128)S(1)} %multiply_reduce_fusion.1), channel_id=1, replica_groups=mesh['zh'=2,'y'=4,'x'=4,'zl'=8,'c'=2] {'zl','c'}, use_global_device_ids=true, to_apply=%region_8.9 | all-reduce | flops 128 | bytes 1024 | tf_op jit(solution)/shard_map/psum | solution.py:139
  254.0 0.1 multiply_convert_fusion
  254.2 0.2 reshape.333
  254.4 2.4 scatter_custom_fusion
  256.9 30.0 %all_to_all.10 = bf16[32,20,180]{2,1,0:T(8,128)(2,1)S(1)} all-to-all(bf16[32,20,180]{2,1,0:T(8,128)(2,1)S(1)} %reshape.312), channel_id=1, replica_groups=mesh['zh'=2,'y'=4,'x'=4,'zl'=8,'c'=2] {'zh','y','x'}, dimensions={0} | all-to-all | bytes 460800 | tf_op jit(solution)/shard_map/all_to_all | solution.py:160
  286.9 0.1 all_gather_reshape.3
  287.1 0.8 copy.78
  288.0 62.0 %all-gather.7.cloned.1.call-done = bf16[8,640,180]{1,2,0:T(8,128)(2,1)} async-done(((bf16[1,640,180]{1,2,0:T(8,128)(2,1)}), bf16[8,640,180]{1,2,0:T(8,128)(2,1)}) %all-gather.7.cloned.1.call-update) | async-done | bytes 1843216 | tf_op jit(solution)/shard_map/all_gather | solution.py:167
  349.9 3.0 copy.79
  353.0 0.2 reduce-scatter.13.cloned.1.call-start
  353.2 1.8 copy.81
  355.0 9.8 %reshape.313 = bf16[8,2,180,360]{2,1,0,3:T(2,128)(2,1)} reshape(bf16[1,2880,2,180]{1,3,2,0:T(8,128)(2,1)S(1)} %copy.81) | data formatting | bytes 4147200 | tf_op jit(solution)/shard_map/reshape | solution.py:169
  364.8 6.4 %reshape.314 = bf16[180,8,2,180]{3,2,1,0:T(2,128)(2,1)S(1)} reshape(bf16[1,180,2880]{2,1,0:T(8,128)(2,1)} %param.23) | data formatting | bytes 2073600 | tf_op jit(solution)/shard_map/reshape | solution.py:179
  371.2 5.6 %all-gather.9.cloned.1.call-done = bf16[16,640,180]{1,0,2:T(8,128)(2,1)} async-done(((bf16[8,640,180]{1,0,2:T(8,128)(2,1)}), bf16[16,640,180]{1,0,2:T(8,128)(2,1)}) %all-gather.9.cloned.1.call-update) | async-done | bytes 3686416 | tf_op jit(solution)/shard_map/all_gather | solution.py:168
  376.8 3.0 copy.80
  379.8 3.0 fusion.8
  382.9 1.8 convert_bitcast_fusion
  384.7 2.6 copy.85
  387.3 0.3 reduce-scatter.17.cloned.1.call-start
  387.5 23.2 %reduce-scatter.13.cloned.1.call-done = bf16[1,8,640,180]{2,1,3,0:T(8,128)(2,1)} async-done(((bf16[2,8,640,180]{2,1,3,0:T(8,128)(2,1)}), bf16[1,8,640,180]{2,1,3,0:T(8,128)(2,1)}) %reduce-scatter.13.cloned.1.call-update) | async-done | bytes 1843216 | tf_op jit(solution)/shard_map/reduce_scatter | solution.py:183
  410.8 3.0 copy.86
  413.8 69.3 %reduce-scatter.17.cloned.1.call-done = bf16[1,640,180]{1,2,0:T(8,128)(2,1)} async-done(((bf16[8,640,180]{1,2,0:T(8,128)(2,1)}), bf16[1,640,180]{1,2,0:T(8,128)(2,1)}) %reduce-scatter.17.cloned.1.call-update) | async-done | bytes 230416
  483.1 1.1 copy.87
  484.2 0.8 reshape_squeeze.3
  485.0 17.0 %all-to-all-start.1 = ((bf16[32,20,180]{2,1,0:T(8,128)(2,1)}), bf16[32,20,180]{2,1,0:T(8,128)(2,1)S(1)}, u32[]{:S(2)}, u32[]{:S(2)}) async-start(bf16[32,20,180]{2,1,0:T(8,128)(2,1)} %reshape_squeeze.3), calls=%async_computation.3 | async-start | bytes 786432 | tf_op jit(solution)/shard_map/all_to_all | solution.py:185
  502.0 0.1 copy.88
  502.1 0.1 reshape.323
  502.2 0.1 copy.72
  502.3 22.2 %all-to-all-done.1 = bf16[32,20,180]{2,1,0:T(8,128)(2,1)S(1)} async-done(((bf16[32,20,180]{2,1,0:T(8,128)(2,1)}), bf16[32,20,180]{2,1,0:T(8,128)(2,1)S(1)}, u32[]{:S(2)}, u32[]{:S(2)}) %all-to-all-start.1) | async-done | bytes 230432 | tf_op jit(solution)/shard_map/all_to_all | solution.py:185
  524.5 0.1 reshape.315
  524.6 2.0 gather_fusion
  526.6 0.2 reshape.340
  526.8 0.4 multiply_reduce_fusion
  527.2 0.7 copy.89
  (44 shorter events, 1.0 us)
Async XLA Ops:
  6.5 122.5 %copy-start = (bf16[128,2880]{0,1:T(8,128)(2,1)S(1)}, bf16[128,2880]{0,1:T(8,128)(2,1)}, u32[]{:S(2)}) copy-start(bf16[128,2880]{0,1:T(8,128)(2,1)} %param.18) | copy-start | bytes 2211844
  6.5 119.7 %copy-start.5 = (f32[2]{0:T(128)S(1)}, f32[2]{0:T(128)}, u32[]{:S(2)}) copy-start(f32[2]{0:T(128)} %param.17) | copy-start | bytes 28
  6.5 117.7 %all-gather.5.cloned.1.call-start = ((), (), s32[]{:S(2)}) async-start(), calls=%async_computation.6 | async-start | bytes 1081344 | tf_op jit(solution)/shard_map/all_gather | solution.py:108
  9.2 138.3 %reduce-scatter.11.cloned.1.call-start = ((), (), s32[]{:S(2)}) async-start(), calls=%async_computation.7 | async-start | bytes 1105920 | tf_op jit(solution)/shard_map/reduce_scatter | solution.py:134
  124.3 2.7 copy-start.2
  129.1 1.6 copy-start.3
  130.7 78.0 %reduce-scatter.15.cloned.1.call-start = ((), (), s32[]{:S(2)}) async-start(), calls=%async_computation.11 | async-start | bytes 423936
  149.3 200.7 %all-gather.7.cloned.1.call-start = ((), (), s32[]{:S(2)}) async-start(), calls=%async_computation.8 | async-start | bytes 2119680 | tf_op jit(solution)/shard_map/all_gather | solution.py:167
  287.9 88.9 %all-gather.9.cloned.1.call-start = ((), (), s32[]{:S(2)}) async-start(), calls=%async_computation.10 | async-start | bytes 5529600 | tf_op jit(solution)/shard_map/all_gather | solution.py:168
  353.0 57.8 %reduce-scatter.13.cloned.1.call-start = ((), (), s32[]{:S(2)}) async-start(), calls=%async_computation.9 | async-start | bytes 5529600 | tf_op jit(solution)/shard_map/reduce_scatter | solution.py:183
  376.8 3.0 copy-start.1
  387.3 95.8 %reduce-scatter.17.cloned.1.call-start = ((), (), s32[]{:S(2)}) async-start(), calls=%async_computation.12 | async-start | bytes 2119680
  410.8 91.4 %copy-start.4 = (f32[128,4]{0,1:T(4,128)S(1)}, f32[128,4]{0,1:T(4,128)}, u32[]{:S(2)}) copy-start(f32[128,4]{0,1:T(4,128)} %param.21) | copy-start | bytes 6148
  485.0 39.5 %all-to-all-start.1 = ((bf16[32,20,180]{2,1,0:T(8,128)(2,1)}), bf16[32,20,180]{2,1,0:T(8,128)(2,1)S(1)}, u32[]{:S(2)}, u32[]{:S(2)}) async-start(bf16[32,20,180]{2,1,0:T(8,128)(2,1)} %reshape_squeeze.3), calls=%async_computation.3 | async-start | bytes 786432 | tf_op jit(solution)/shard_map/all_to_all | solution.py:185
Sparse Core Ops, SparseCore 0:
  11.4 112.7 all-gather.4
  130.8 16.6 reduce-scatter.10
  150.3 58.3 reduce-scatter.14
  288.1 61.8 all-gather.6
  353.1 23.7 all-gather.8
  387.4 23.3 reduce-scatter.12
  413.9 69.0 reduce-scatter.16
where the time goes:
time: 535 us
  waiting for transfers between devices  367 us (69%)
  blocking collectives  74.4 us (14%)
  local copies, waits for them, and re-layouts  46.9 us (9%)
  starting transfers between devices  17.6 us (3%)
  between operations  13.8 us (3%)
  matrix products  9.28 us (2%)
    unnamed x9, waiting for transfers between devices  125 us
    all_gather x1, waiting for transfers between devices, per_device(): block_part = lax.all_gather(key_value, CTX, axis=0, tiled=True)  113 us
    all_gather x1, waiting for transfers between devices, per_device(): gathered = lax.all_gather(received, 'zl', axis=0, tiled=False)  62 us
    psum x1, blocking collectives, per_device(): square_sum = lax.psum(jnp.sum(residual_cols * residual_cols, axis=1), EXP)  44.4 us
    all_to_all x1, blocking collectives, per_device(): lax.all_to_all(send_rows.reshape(ctx_count, exp_local * capacity, col_wid...  30 us
    reduce_scatter x1, waiting for transfers between devices, per_device(): lax.psum_scatter(partial_value, 'c', scatter_dimension=0, tiled=True)[0]  23.2 us
    all_to_all x1, waiting for transfers between devices, per_device(): lax.all_to_all(expert_cols.reshape(ctx_count, capacity, col_width), CTX,...  22.2 us
    all_to_all x1, starting transfers between devices, per_device(): lax.all_to_all(expert_cols.reshape(ctx_count, capacity, col_width), CTX,...  17 us
  transfers between devices with their start and end apart: 8, of which 8 were waited for; matrix products, arithmetic and copies ran while one was open for 5% of the time, Pallas kernels for 0%

commit v1 on v0

--- a/solution.py
+++ b/solution.py
@@ -105,7 +105,19 @@
     )
     key_value = jnp.concatenate([key_rot, value_block], axis=1)
     score_scale = 1.0 / math.sqrt(HEAD_SIZE)
-    block_part = lax.all_gather(key_value, CTX, axis=0, tiled=True)
+
+    def plan_the_meshes(unit, row_axis):
+        return jnp.concatenate(
+            lax.all_to_all(
+                jnp.stack([unit] * lax.psum(1, axis_name=row_axis)),
+                axis_name=row_axis,
+                split_axis=0,
+                concat_axis=0,
+            ),
+            axis=0,
+        )
+
+    block_part = plan_the_meshes(key_value, CTX)
     run_max = jnp.broadcast_to(sink_logits[:, None], (local_heads, tok_rows))
     run_total = jnp.ones((local_heads, tok_rows), jnp.float32)
     key_count = block_part.shape[0]

time: 535 us -> 492 us (0.920)
  waiting for transfers between devices: 367 us -> 305 us
  starting transfers between devices: 17.6 us -> 37.2 us
    all_gather x1 -> x0, waiting for transfers between devices: 113 us -> none  [per_device(): block_part = lax.all_gather(key_value, CTX, axis=0, tiled=True)]
    all_to_all x0 -> x1, waiting for transfers between devices: none -> 57.2 us  [plan_the_meshes(): lax.all_to_all(jnp.stack([unit] * lax.psum(1, axis_name=row_axis)), axis_...]
    all_to_all x0 -> x1, starting transfers between devices: none -> 19.7 us  [plan_the_meshes(): lax.all_to_all(jnp.stack([unit] * lax.psum(1, axis_name=row_axis)), axis_...]
    reduce_scatter x1, waiting for transfers between devices: 16.4 us -> 10.2 us  [per_device(): lax.psum_scatter(head_part, 'c', scatter_dimension=0, tiled=True)[0]]
    unnamed x9 -> x8, waiting for transfers between devices: 125 us -> 126 us
where the time goes in v1:
time: 492 us; the launch traced here: 491 us
  waiting for transfers between devices  305 us (62%)
  blocking collectives  74.1 us (15%)
  local copies, waits for them, and re-layouts  48.3 us (10%)
  starting transfers between devices  37.2 us (8%)
  between operations  13.9 us (3%)
  matrix products  8.15 us (2%)
    unnamed x8, waiting for transfers between devices  126 us
    all_gather x1, waiting for transfers between devices, per_device(): gathered = lax.all_gather(received, 'zl', axis=0, tiled=False)  61.3 us
    all_to_all x1, waiting for transfers between devices, plan_the_meshes(): lax.all_to_all(jnp.stack([unit] * lax.psum(1, axis_name=row_axis)), axis_...  57.2 us
    psum x1, blocking collectives, per_device(): square_sum = lax.psum(jnp.sum(residual_cols * residual_cols, axis=1), EXP)  44 us
    all_to_all x1, blocking collectives, per_device(): lax.all_to_all(send_rows.reshape(ctx_count, exp_local * capacity, col_wid...  30.1 us
    reduce_scatter x1, waiting for transfers between devices, per_device(): lax.psum_scatter(partial_value, 'c', scatter_dimension=0, tiled=True)[0]  23.2 us
    all_to_all x1, waiting for transfers between devices, per_device(): lax.all_to_all(expert_cols.reshape(ctx_count, capacity, col_width), CTX,...  22.2 us
    all_to_all x1, starting transfers between devices, plan_the_meshes(): lax.all_to_all(jnp.stack([unit] * lax.psum(1, axis_name=row_axis)), axis_...  19.7 us
  transfers between devices with their start and end apart: 8, of which 8 were waited for; matrix products, arithmetic and copies ran while one was open for 5% of the time, Pallas kernels for 0%

profile of v1, /device:TPU:32, one launch (start us, length us, event | category | flops | bytes accessed | tf_op | source)
XLA Modules:
  0.0 490.9 jit_solution(6888082760616898453)
XLA Ops:
  6.5 0.9 constant_dynamic-slice_fusion
  7.7 0.8 fusion.33
  8.5 1.2 stack.2
  9.8 19.7 %all-to-all-start = ((bf16[32,128,128]{1,2,0:T(8,128)(2,1)}), bf16[32,128,128]{1,2,0:T(8,128)(2,1)S(1)}, u32[]{:S(2)}, u32[]{:S(2)}) async-start(bf16[32,128,128]{1,2,0:T(8,128)(2,1)} %stack.2), calls=%async_computation | async-start | bytes 2097152 | tf_op jit(solution)/shard_map/all_to_all | solution.py:111
  29.5 0.8 copy.66
  30.4 0.1 fusion.39
  30.6 0.3 iota_compare_fusion
  30.9 57.2 %all-to-all-done = bf16[32,128,128]{1,2,0:T(8,128)(2,1)S(1)} async-done(((bf16[32,128,128]{1,2,0:T(8,128)(2,1)}), bf16[32,128,128]{1,2,0:T(8,128)(2,1)S(1)}, u32[]{:S(2)}, u32[]{:S(2)}) %all-to-all-start) | async-done | bytes 1048608 | tf_op jit(solution)/shard_map/all_to_all | solution.py:111
  88.1 0.1 copy_bitcast_fusion
  88.3 0.9 fusion.45
  89.3 0.6 fusion.2
  89.9 2.1 fusion.13
  92.0 0.3 convolution_convert_fusion
  92.3 0.1 reshape.313
  92.5 1.1 copy.68
  93.6 0.1 copy.72
  93.7 0.1 eq.29
  93.8 0.1 eq.25
  94.0 10.2 %reduce-scatter.11.cloned.1.call-done = bf16[1,8,128,180]{2,1,3,0:T(8,128)(2,1)} async-done(((bf16[2,8,128,180]{2,1,3,0:T(8,128)(2,1)}), bf16[1,8,128,180]{2,1,3,0:T(8,128)(2,1)}) %reduce-scatter.11.cloned.1.call-update) | async-done | bytes 368656 | tf_op jit(solution)/shard_map/reduce_scatter | solution.py:146
  104.1 1.8 copy.69
  106.0 0.8 constant_dynamic-slice_fusion.2
  106.9 0.8 dynamic_slice.15
  107.7 1.1 reduce-window.6
  108.8 0.2 slice_reduce_fusion
  109.1 0.1 fusion.24
  109.2 0.1 reshape.315
  109.4 0.1 copy.76
  109.5 0.1 reshape.316
  109.7 56.1 %reduce-scatter.15.cloned.1.call-done = bf16[1,128,180]{1,2,0:T(8,128)(2,1)} async-done(((bf16[8,128,180]{1,2,0:T(8,128)(2,1)}), bf16[1,128,180]{1,2,0:T(8,128)(2,1)}) %reduce-scatter.15.cloned.1.call-update) | async-done | bytes 46096
  165.7 0.9 copy.70
  166.6 0.1 multiply_reduce_fusion.1
  166.7 44.0 %psum.7 = f32[128]{0:T(128)S(1)} all-reduce(f32[128]{0:T(128)S(1)} %multiply_reduce_fusion.1), channel_id=1, replica_groups=mesh['zh'=2,'y'=4,'x'=4,'zl'=8,'c'=2] {'zl','c'}, use_global_device_ids=true, to_apply=%region_8.9 | all-reduce | flops 128 | bytes 1024 | tf_op jit(solution)/shard_map/psum | solution.py:151
  210.9 0.2 reshape.339
  211.0 2.4 scatter_custom_fusion
  213.5 30.1 %all_to_all.15 = bf16[32,20,180]{2,1,0:T(8,128)(2,1)S(1)} all-to-all(bf16[32,20,180]{2,1,0:T(8,128)(2,1)S(1)} %reshape.318), channel_id=1, replica_groups=mesh['zh'=2,'y'=4,'x'=4,'zl'=8,'c'=2] {'zh','y','x'}, dimensions={0} | all-to-all | bytes 460800 | tf_op jit(solution)/shard_map/all_to_all | solution.py:172
  243.6 0.1 all_gather_reshape.3
  243.8 0.8 copy.77
  244.7 61.3 %all-gather.4.cloned.1.call-done = bf16[8,640,180]{1,2,0:T(8,128)(2,1)} async-done(((bf16[1,640,180]{1,2,0:T(8,128)(2,1)}), bf16[8,640,180]{1,2,0:T(8,128)(2,1)}) %all-gather.4.cloned.1.call-update) | async-done | bytes 1843216 | tf_op jit(solution)/shard_map/all_gather | solution.py:179
  306.0 3.0 copy.78
  309.1 0.2 reduce-scatter.13.cloned.1.call-start
  309.3 1.8 copy.80
  311.1 9.8 %reshape.319 = bf16[8,2,180,360]{2,1,0,3:T(2,128)(2,1)} reshape(bf16[1,2880,2,180]{1,3,2,0:T(8,128)(2,1)S(1)} %copy.80) | data formatting | bytes 4147200 | tf_op jit(solution)/shard_map/reshape | solution.py:181
  320.9 6.4 %reshape.320 = bf16[180,8,2,180]{3,2,1,0:T(2,128)(2,1)S(1)} reshape(bf16[1,180,2880]{2,1,0:T(8,128)(2,1)} %param.23) | data formatting | bytes 2073600 | tf_op jit(solution)/shard_map/reshape | solution.py:191
  327.3 5.6 %all-gather.6.cloned.1.call-done = bf16[16,640,180]{1,0,2:T(8,128)(2,1)} async-done(((bf16[8,640,180]{1,0,2:T(8,128)(2,1)}), bf16[16,640,180]{1,0,2:T(8,128)(2,1)}) %all-gather.6.cloned.1.call-update) | async-done | bytes 3686416 | tf_op jit(solution)/shard_map/all_gather | solution.py:180
  332.9 3.0 copy.79
  335.9 3.0 fusion.8
  338.9 1.8 convert_bitcast_fusion
  340.8 2.6 copy.84
  343.3 0.3 reduce-scatter.17.cloned.1.call-start
  343.6 23.2 %reduce-scatter.13.cloned.1.call-done = bf16[1,8,640,180]{2,1,3,0:T(8,128)(2,1)} async-done(((bf16[2,8,640,180]{2,1,3,0:T(8,128)(2,1)}), bf16[1,8,640,180]{2,1,3,0:T(8,128)(2,1)}) %reduce-scatter.13.cloned.1.call-update) | async-done | bytes 1843216 | tf_op jit(solution)/shard_map/reduce_scatter | solution.py:195
  366.9 3.0 copy.85
  369.9 69.4 %reduce-scatter.17.cloned.1.call-done = bf16[1,640,180]{1,2,0:T(8,128)(2,1)} async-done(((bf16[8,640,180]{1,2,0:T(8,128)(2,1)}), bf16[1,640,180]{1,2,0:T(8,128)(2,1)}) %reduce-scatter.17.cloned.1.call-update) | async-done | bytes 230416
  439.3 1.1 copy.86
  440.4 0.8 reshape_squeeze.3
  441.2 16.9 %all-to-all-start.2 = ((bf16[32,20,180]{2,1,0:T(8,128)(2,1)}), bf16[32,20,180]{2,1,0:T(8,128)(2,1)S(1)}, u32[]{:S(2)}, u32[]{:S(2)}) async-start(bf16[32,20,180]{2,1,0:T(8,128)(2,1)} %reshape_squeeze.3), calls=%async_computation.4 | async-start | bytes 786432 | tf_op jit(solution)/shard_map/all_to_all | solution.py:197
  458.1 0.1 copy.87
  458.3 0.1 reshape.329
  458.4 0.1 copy.71
  458.5 22.2 %all-to-all-done.2 = bf16[32,20,180]{2,1,0:T(8,128)(2,1)S(1)} async-done(((bf16[32,20,180]{2,1,0:T(8,128)(2,1)}), bf16[32,20,180]{2,1,0:T(8,128)(2,1)S(1)}, u32[]{:S(2)}, u32[]{:S(2)}) %all-to-all-start.2) | async-done | bytes 230432 | tf_op jit(solution)/shard_map/all_to_all | solution.py:197
  480.7 0.1 reshape.321
  480.8 2.0 gather_fusion
  482.8 0.2 reshape.346
  482.9 0.4 multiply_reduce_fusion
  483.3 0.7 copy.88
  (45 shorter events, 1.2 us)
Async XLA Ops:
  6.5 85.5 %copy-start = (bf16[128,2880]{0,1:T(8,128)(2,1)S(1)}, bf16[128,2880]{0,1:T(8,128)(2,1)}, u32[]{:S(2)}) copy-start(bf16[128,2880]{0,1:T(8,128)(2,1)} %param.18) | copy-start | bytes 2211844
  6.5 23.8 %copy-start.3 = (f32[32]{0:T(128)S(1)}, f32[32]{0:T(128)}, u32[]{:S(2)}) copy-start(f32[32]{0:T(128)} %constant.89.clone) | copy-start | bytes 388
  9.8 78.4 %all-to-all-start = ((bf16[32,128,128]{1,2,0:T(8,128)(2,1)}), bf16[32,128,128]{1,2,0:T(8,128)(2,1)S(1)}, u32[]{:S(2)}, u32[]{:S(2)}) async-start(bf16[32,128,128]{1,2,0:T(8,128)(2,1)} %stack.2), calls=%async_computation | async-start | bytes 2097152 | tf_op jit(solution)/shard_map/all_to_all | solution.py:111
  29.5 74.7 %reduce-scatter.11.cloned.1.call-start = ((), (), s32[]{:S(2)}) async-start(), calls=%async_computation.7 | async-start | bytes 1105920 | tf_op jit(solution)/shard_map/reduce_scatter | solution.py:146
  30.9 58.3 %copy-start.5 = (f32[2]{0:T(128)S(1)}, f32[2]{0:T(128)}, u32[]{:S(2)}) copy-start(f32[2]{0:T(128)} %param.17) | copy-start | bytes 28
  92.0 1.6 copy-start.2
  93.6 72.2 %reduce-scatter.15.cloned.1.call-start = ((), (), s32[]{:S(2)}) async-start(), calls=%async_computation.11 | async-start | bytes 423936
  105.9 200.1 %all-gather.4.cloned.1.call-start = ((), (), s32[]{:S(2)}) async-start(), calls=%async_computation.8 | async-start | bytes 2119680 | tf_op jit(solution)/shard_map/all_gather | solution.py:179
  244.6 88.3 %all-gather.6.cloned.1.call-start = ((), (), s32[]{:S(2)}) async-start(), calls=%async_computation.10 | async-start | bytes 5529600 | tf_op jit(solution)/shard_map/all_gather | solution.py:180
  309.1 57.8 %reduce-scatter.13.cloned.1.call-start = ((), (), s32[]{:S(2)}) async-start(), calls=%async_computation.9 | async-start | bytes 5529600 | tf_op jit(solution)/shard_map/reduce_scatter | solution.py:195
  332.9 3.0 copy-start.1
  343.3 95.9 %reduce-scatter.17.cloned.1.call-start = ((), (), s32[]{:S(2)}) async-start(), calls=%async_computation.12 | async-start | bytes 2119680
  366.9 91.5 %copy-start.4 = (f32[128,4]{0,1:T(4,128)S(1)}, f32[128,4]{0,1:T(4,128)}, u32[]{:S(2)}) copy-start(f32[128,4]{0,1:T(4,128)} %param.21) | copy-start | bytes 6148
  441.2 39.4 %all-to-all-start.2 = ((bf16[32,20,180]{2,1,0:T(8,128)(2,1)}), bf16[32,20,180]{2,1,0:T(8,128)(2,1)S(1)}, u32[]{:S(2)}, u32[]{:S(2)}) async-start(bf16[32,20,180]{2,1,0:T(8,128)(2,1)} %reshape_squeeze.3), calls=%async_computation.4 | async-start | bytes 786432 | tf_op jit(solution)/shard_map/all_to_all | solution.py:197
Sparse Core Ops, SparseCore 0:
  93.7 10.3 reduce-scatter.10
  106.9 58.7 reduce-scatter.14
  244.8 61.2 all-gather.3
  309.2 23.6 all-gather.5
  343.5 23.3 reduce-scatter.12
  370.0 69.2 reduce-scatter.16
